TPU v7x, 32 devices: a whole 2x2x4 slice. The times are simulated.
32 devices in a mesh: dp: 8 (over y, x, core), tensor: 4 (over z).
Axes of the slice: x: 2, y: 2, z: 4, core: 2. Of those that a mesh axis runs over, the one named last changes fastest.
Arguments:
- inputs: bfloat16 [16384, 768], P(('dp', 'tensor')), may hold values from -6 to 6
- cotangent: bfloat16 [16384, 768], P(('dp', 'tensor')), may hold values from -6 to 6
- lengths: int32 [128], P('dp'), may hold values from 25 to 128
- block_kind: int32 [32], P('dp'), may hold values from 0 to 1
- w_qkv: bfloat16 [2, 3, 768, 768], P(None, None, None, 'tensor'), may hold values from -0.3125 to 0.3125
- qv_bias: bfloat16 [2, 2, 768], P(None, None, 'tensor'), may hold values from -3 to 3
- w_out: bfloat16 [2, 768, 768], P(None, 'tensor'), may hold values from -0.625 to 0.625
- resid_bias: bfloat16 [2, 2, 768], replicated, may hold values from -3 to 3
- norm_gain: bfloat16 [2, 2, 768], replicated, may hold values from 0.5 to 1.5
- norm_shift: bfloat16 [2, 2, 768], replicated, may hold values from -2 to 2
- w_up: bfloat16 [2, 768, 3072], P(None, None, 'tensor'), may hold values from -0.21875 to 0.21875
- up_bias: bfloat16 [2, 3072], P(None, 'tensor'), may hold values from -3 to 3
- w_down: bfloat16 [2, 3072, 768], P(None, 'tensor'), may hold values from -0.15625 to 0.15625
Outputs:
- layer_out: bfloat16 [16384, 768], P(('dp', 'tensor'))
- input_grad: float32 [16384, 768], P(('dp', 'tensor'))
- grad_w_qkv: float32 [2, 3, 768, 768], P(None, None, None, 'tensor')
- grad_qv_bias: float32 [2, 2, 768], P(None, None, 'tensor')
- grad_w_out: float32 [2, 768, 768], P(None, 'tensor')
- grad_resid_bias: float32 [2, 2, 768], replicated
- grad_norm_gain: float32 [2, 2, 768], replicated
- grad_norm_shift: float32 [2, 2, 768], replicated
- grad_w_up: float32 [2, 768, 3072], P(None, None, 'tensor')
- grad_up_bias: float32 [2, 3072], P(None, 'tensor')
- grad_w_down: float32 [2, 3072, 768], P(None, 'tensor')
Inputs may be any that keep to these rules, and one draw needn't show every extreme that they name: lengths[s] is the number of real tokens of chain s; positions from lengths[s] on are padding and are never attended to. `block_kind`: block b holds chains b * 4 to (b+1) * 4 - 1, all heavy (0) or all light (1).
All inputs are finite; a program needn't handle non-finite values.
Results may differ from a plain program's by a relative error of at most 0.019.
The roundings to bfloat16 on the way count: a program that leaves them out, or rounds other values in their place, can miss the bound.
Values may be sent and summed in bfloat16 or wider, within the bound.
No kernel may reach another device: no remote copies, remote signals or barrier semaphores. Data moves between devices by JAX's collectives and lax.ppermute only.
A program may use at most 128 MiB of HBM per device.

v0:
```python
import jax
import jax.numpy as jnp
from jax import lax
from jax.sharding import PartitionSpec as P

HEAD_DIM = 64
CHAIN = 128
BLOCK_SEQS = 4
EPSILON = 1e-05
SQRT_HALF = 0.7071067811865476
INV_ROOT_TWO_PI = 0.3989422804014327


def norm_forward(row_data, gain_rows, shift_rows):
    mean_row = jnp.mean(row_data, axis=-1, keepdims=True)
    centred = row_data - mean_row
    var_row = jnp.mean(centred * centred, axis=-1, keepdims=True)
    inv_std = lax.rsqrt(var_row + EPSILON)
    unit_rows = centred * inv_std
    return (unit_rows * gain_rows + shift_rows, unit_rows, inv_std)


def norm_backward(grad_rows, gain_rows, unit_rows, inv_std):
    scaled = grad_rows * gain_rows
    mean_first = jnp.mean(scaled, axis=-1, keepdims=True)
    mean_second = jnp.mean(scaled * unit_rows, axis=-1, keepdims=True)
    return inv_std * (scaled - mean_first - unit_rows * mean_second)


def type_sum(kind_hot, values):
    return jnp.einsum("rt,rd->td", kind_hot, values, precision=lax.Precision.HIGHEST)


def gelu_slope(values):
    return 0.5 * (1.0 + lax.erf(values * SQRT_HALF)) + values * INV_ROOT_TWO_PI * jnp.exp(
        -0.5 * values * values
    )


def split_heads(row_data, heads_here):
    return row_data.reshape(BLOCK_SEQS, CHAIN, heads_here, HEAD_DIM)


def ffn_apply(up_w, ubias_w, down_w, row_blocks, kinds):

    def step(carry, packed):
        row_data, block_type = packed
        pre_act = jnp.dot(row_data, up_w[block_type], preferred_element_type=jnp.float32) + ubias_w[
            block_type
        ].astype(jnp.float32)
        activ = jax.nn.gelu(pre_act, approximate=False).astype(jnp.bfloat16)
        return (
            carry,
            (
                pre_act,
                activ,
                jnp.dot(activ, down_w[block_type], preferred_element_type=jnp.float32),
            ),
        )

    return lax.scan(step, 0, (row_blocks, kinds))[1]


def ffn_grad(up_w, ubias_w, down_w, row_blocks, grad_blocks, pre_blocks, activ_blocks, kinds):

    def step(accums, packed):
        acc_up, acc_ubias, acc_down = accums
        row_data, grad_rows, pre_act, activ, block_type = packed
        acc_down = acc_down.at[block_type].add(
            jnp.einsum("rf,rd->fd", activ, grad_rows, preferred_element_type=jnp.float32)
        )
        d_activ = jnp.einsum(
            "rd,fd->rf", grad_rows, down_w[block_type], preferred_element_type=jnp.float32
        ).astype(jnp.bfloat16)
        d_pre = (d_activ.astype(jnp.float32) * gelu_slope(pre_act)).astype(jnp.bfloat16)
        acc_up = acc_up.at[block_type].add(
            jnp.einsum("rd,rf->df", row_data, d_pre, preferred_element_type=jnp.float32)
        )
        acc_ubias = acc_ubias.at[block_type].add(jnp.sum(d_pre.astype(jnp.float32), axis=0))
        partial_back = jnp.einsum(
            "rf,df->rd", d_pre, up_w[block_type], preferred_element_type=jnp.float32
        )
        return ((acc_up, acc_ubias, acc_down), partial_back)

    zeros_ffn = (
        jnp.zeros(up_w.shape, jnp.float32),
        jnp.zeros(ubias_w.shape, jnp.float32),
        jnp.zeros(down_w.shape, jnp.float32),
    )
    return lax.scan(step, zeros_ffn, (row_blocks, grad_blocks, pre_blocks, activ_blocks, kinds))


def local(
    inputs,
    cotangent,
    lengths,
    block_kind,
    w_qkv,
    qv_bias,
    w_out,
    resid_bias,
    norm_gain,
    norm_shift,
    w_up,
    up_bias,
    w_down,
):
    tok_dev = inputs.shape[0]
    group_rows = tok_dev * lax.axis_size("tensor")
    block_rows = BLOCK_SEQS * CHAIN
    n_blocks = group_rows // block_rows
    heads_here = w_qkv.shape[3] // HEAD_DIM
    score_scale = HEAD_DIM ** (-0.5)
    highest = lax.Precision.HIGHEST
    row_block = (lax.axis_index("tensor") * tok_dev + jnp.arange(tok_dev)) // block_rows
    block_hot = row_block[:, None] == jnp.arange(n_blocks)[None, :]
    row_kind = jnp.sum(jnp.where(block_hot, block_kind[None, :], 0), axis=1)
    kind_hot = (row_kind[:, None] == jnp.arange(2)[None, :]).astype(jnp.float32)

    def pick(kind_table):
        return jnp.dot(kind_hot, kind_table.astype(jnp.float32), precision=highest)

    key_valid = jnp.arange(CHAIN)[None, :] < lengths[:, None]
    valid_blocks = key_valid.reshape(n_blocks, BLOCK_SEQS, CHAIN)

    def scores_of(query_rows, key_rows, valid_keys):
        raw_scores = (
            jnp.einsum(
                "sqhd,skhd->shqk",
                split_heads(query_rows, heads_here),
                split_heads(key_rows, heads_here),
                preferred_element_type=jnp.float32,
            )
            * score_scale
        )
        return jnp.where(valid_keys[:, None, None, :], raw_scores, -1e30)

    gathered = lax.all_gather(inputs, "tensor", axis=0, tiled=True)
    input_blocks = gathered.reshape(n_blocks, block_rows, -1)

    def attend_forward(accums, packed):
        row_data, valid_keys, block_type = packed
        projected = jnp.einsum(
            "rd,jde->jre", row_data, w_qkv[block_type], preferred_element_type=jnp.float32
        )
        bias_pair = qv_bias[block_type].astype(jnp.float32)
        query_rows = (projected[0] + bias_pair[0]).astype(jnp.bfloat16)
        key_rows = projected[1].astype(jnp.bfloat16)
        value_rows = (projected[2] + bias_pair[1]).astype(jnp.bfloat16)
        scores = scores_of(query_rows, key_rows, valid_keys)
        row_max = jnp.max(scores, axis=-1, keepdims=True)
        log_total = row_max[..., 0] + jnp.log(jnp.sum(jnp.exp(scores - row_max), axis=-1))
        attn_probs = jnp.exp(scores - log_total[..., None]).astype(jnp.bfloat16)
        mixed = jnp.einsum(
            "shqk,skhd->sqhd",
            attn_probs,
            split_heads(value_rows, heads_here),
            preferred_element_type=jnp.float32,
        )
        mixed = mixed.reshape(block_rows, -1).astype(jnp.bfloat16)
        partial_out = jnp.dot(mixed, w_out[block_type], preferred_element_type=jnp.float32)
        return (
            accums,
            (jnp.stack([query_rows, key_rows, value_rows]), log_total, mixed, partial_out),
        )

    unused, (kept_proj, kept_total, kept_mixed, attn_parts) = lax.scan(
        attend_forward, 0, (input_blocks, valid_blocks, block_kind)
    )
    attn_rows = lax.psum_scatter(
        attn_parts.reshape(group_rows, -1), "tensor", scatter_dimension=0, tiled=True
    )
    hidden_one = inputs.astype(jnp.float32) + attn_rows + pick(resid_bias[:, 0])
    gain_one = pick(norm_gain[:, 0])
    normed, unit_one, inv_one = norm_forward(hidden_one, gain_one, pick(norm_shift[:, 0]))
    normed_low = normed.astype(jnp.bfloat16)
    gathered_norm = lax.all_gather(normed_low, "tensor", axis=0, tiled=True)
    norm_blocks = gathered_norm.reshape(n_blocks, block_rows, -1)
    kept_pre, kept_activ, ffn_parts = ffn_apply(w_up, up_bias, w_down, norm_blocks, block_kind)
    ffn_rows = lax.psum_scatter(
        ffn_parts.reshape(group_rows, -1), "tensor", scatter_dimension=0, tiled=True
    )
    hidden_two = normed + ffn_rows + pick(resid_bias[:, 1])
    gain_two = pick(norm_gain[:, 1])
    output_rows, unit_two, inv_two = norm_forward(hidden_two, gain_two, pick(norm_shift[:, 1]))
    layer_out = output_rows.astype(jnp.bfloat16)
    grad_out = cotangent.astype(jnp.float32)
    d_two = norm_backward(grad_out, gain_two, unit_two, inv_two)
    d_two_low = d_two.astype(jnp.bfloat16)
    gathered_two = lax.all_gather(d_two_low, "tensor", axis=0, tiled=True)
    two_blocks = gathered_two.reshape(n_blocks, block_rows, -1)
    (acc_up, acc_ubias, acc_down), ffn_back_parts = ffn_grad(
        w_up, up_bias, w_down, norm_blocks, two_blocks, kept_pre, kept_activ, block_kind
    )
    d_normed = (
        lax.psum_scatter(
            ffn_back_parts.reshape(group_rows, -1), "tensor", scatter_dimension=0, tiled=True
        )
        + d_two
    )
    up_total, ubias_total, down_total = (acc_up, acc_ubias, acc_down)
    d_one = norm_backward(d_normed, gain_one, unit_one, inv_one)
    gain_grads = jnp.stack(
        [type_sum(kind_hot, d_normed * unit_one), type_sum(kind_hot, grad_out * unit_two)], axis=1
    )
    shift_grads = jnp.stack([type_sum(kind_hot, d_normed), type_sum(kind_hot, grad_out)], axis=1)
    rbias_grads = jnp.stack([type_sum(kind_hot, d_one), type_sum(kind_hot, d_two)], axis=1)
    gathered_one = lax.all_gather(d_one.astype(jnp.bfloat16), "tensor", axis=0, tiled=True)
    one_blocks = gathered_one.reshape(n_blocks, block_rows, -1)

    def attend_backward(accums, packed):
        acc_qkv, acc_qv, acc_out = accums
        row_data, grad_rows, valid_keys, kept_rows, log_total, mixed, block_type = packed
        acc_out = acc_out.at[block_type].add(
            jnp.einsum("re,rd->ed", mixed, grad_rows, preferred_element_type=jnp.float32)
        )
        d_mixed = jnp.einsum(
            "rd,ed->re", grad_rows, w_out[block_type], preferred_element_type=jnp.float32
        ).astype(jnp.bfloat16)
        scores = scores_of(kept_rows[0], kept_rows[1], valid_keys)
        attn_probs = jnp.exp(scores - log_total[..., None])
        d_mixed_heads = split_heads(d_mixed, heads_here)
        d_value = jnp.einsum(
            "shqk,sqhd->skhd",
            attn_probs.astype(jnp.bfloat16),
            d_mixed_heads,
            preferred_element_type=jnp.float32,
        )
        d_value = d_value.reshape(block_rows, -1).astype(jnp.bfloat16)
        d_probs = jnp.einsum(
            "sqhd,skhd->shqk",
            d_mixed_heads,
            split_heads(kept_rows[2], heads_here),
            preferred_element_type=jnp.float32,
        )
        prob_dot = jnp.sum(attn_probs * d_probs, axis=-1, keepdims=True)
        d_scores = (attn_probs * (d_probs - prob_dot)).astype(jnp.bfloat16)
        d_query = (
            jnp.einsum(
                "shqk,skhd->sqhd",
                d_scores,
                split_heads(kept_rows[1], heads_here),
                preferred_element_type=jnp.float32,
            )
            * score_scale
        )
        d_key = (
            jnp.einsum(
                "shqk,sqhd->skhd",
                d_scores,
                split_heads(kept_rows[0], heads_here),
                preferred_element_type=jnp.float32,
            )
            * score_scale
        )
        d_query = d_query.reshape(block_rows, -1).astype(jnp.bfloat16)
        d_key = d_key.reshape(block_rows, -1).astype(jnp.bfloat16)
        d_proj = jnp.stack([d_query, d_key, d_value])
        acc_qkv = acc_qkv.at[block_type].add(
            jnp.einsum("rd,jre->jde", row_data, d_proj, preferred_element_type=jnp.float32)
        )
        bias_sums = jnp.stack(
            [
                jnp.sum(d_query.astype(jnp.float32), axis=0),
                jnp.sum(d_value.astype(jnp.float32), axis=0),
            ]
        )
        acc_qv = acc_qv.at[block_type].add(bias_sums)
        partial_back = jnp.einsum(
            "jre,jde->rd", d_proj, w_qkv[block_type], preferred_element_type=jnp.float32
        )
        return ((acc_qkv, acc_qv, acc_out), partial_back)

    zeros_attn = (
        jnp.zeros(w_qkv.shape, jnp.float32),
        jnp.zeros(qv_bias.shape, jnp.float32),
        jnp.zeros(w_out.shape, jnp.float32),
    )
    (acc_qkv, acc_qv, acc_out), qkv_back_parts = lax.scan(
        attend_backward,
        zeros_attn,
        (input_blocks, one_blocks, valid_blocks, kept_proj, kept_total, kept_mixed, block_kind),
    )
    input_grad = (
        lax.psum_scatter(
            qkv_back_parts.reshape(group_rows, -1).astype(jnp.bfloat16),
            "tensor",
            scatter_dimension=0,
            tiled=True,
        ).astype(jnp.float32)
        + d_one
    )
    qkv_total, qv_total, out_total, up_total, ubias_total, down_total = lax.psum(
        (acc_qkv, acc_qv, acc_out, up_total, ubias_total, down_total), "dp"
    )
    rbias_total, gain_total, shift_total = lax.psum(
        (rbias_grads, gain_grads, shift_grads), ("dp", "tensor")
    )
    return (
        layer_out,
        input_grad,
        qkv_total,
        qv_total,
        out_total,
        rbias_total,
        gain_total,
        shift_total,
        up_total,
        ubias_total,
        down_total,
    )


def solution(mesh):
    return jax.shard_map(
        local,
        mesh=mesh,
        in_specs=(
            P(("dp", "tensor"), None),
            P(("dp", "tensor"), None),
            P("dp"),
            P("dp"),
            P(None, None, None, "tensor"),
            P(None, None, "tensor"),
            P(None, "tensor", None),
            P(),
            P(),
            P(),
            P(None, None, "tensor"),
            P(None, "tensor"),
            P(None, "tensor", None),
        ),
        out_specs=(
            P(("dp", "tensor"), None),
            P(("dp", "tensor"), None),
            P(None, None, None, "tensor"),
            P(None, None, "tensor"),
            P(None, "tensor", None),
            P(),
            P(),
            P(),
            P(None, None, "tensor"),
            P(None, "tensor"),
            P(None, "tensor", None),
        ),
        check_vma=False,
    )
```

profile of v0, /device:TPU:0, one launch (start us, length us, event | category | flops | bytes accessed | tf_op | source)
XLA Modules:
  0.0 1168.2 jit_solution(15813986910202748736)
XLA Ops:
  8.8 67.0 %all-gather.5.cloned.1.call-done = bf16[2048,768]{1,0:T(8,128)(2,1)} async-done(((bf16[512,768]{1,0:T(8,128)(2,1)}), bf16[2048,768]{1,0:T(8,128)(2,1)}) %all-gather.5.cloned.1.call-update) | async-done | bytes 3145744 | tf_op jit(solution)/shard_map/all_gather | solution.py:138
  75.8 3.2 broadcast.348.clone
  79.0 39.6 %while.68 = (s32[]{:T(128)}, bf16[4,3,512,192]{2,3,1,0:T(8,128)(2,1)}, f32[4,4,3,128]{3,2,1,0:T(4,128)S(1)}, bf16[4,512,192]{1,2,0:T(8,128)(2,1)S(1)}, f32[4,512...) while((s32[]{:T(128)}, ...), condition=%wide.region_3.4_spmd, body=%wide.region_0.3_spmd.sunk | while | flops 658340736 | bytes 15210975 | solution.py:167
  120.6 107.5 %reduce-scatter.5.cloned.1.call-done = f32[512,768]{1,0:T(8,128)} async-done(((f32[2048,768]{1,0:T(8,128)}), f32[512,768]{1,0:T(8,128)}) %reduce-scatter.5.cloned.1.call-update) | async-done | bytes 1572880 | tf_op jit(solution)/shard_map/reduce_scatter | solution.py:170
  232.6 64.0 %all-gather.7.cloned.1.call-done = bf16[2048,768]{1,0:T(8,128)(2,1)} async-done(((bf16[512,768]{1,0:T(8,128)(2,1)}), bf16[2048,768]{1,0:T(8,128)(2,1)}) %all-gather.7.cloned.1.call-update) | async-done | bytes 3145744 | tf_op jit(solution)/shard_map/all_gather | solution.py:177
  296.6 3.2 broadcast.348.clone.1
  299.8 3.1 broadcast.348.clone.2
  303.0 48.6 %while.69 = (s32[]{:T(128)}, f32[4,512,768]{2,1,0:T(8,128)}, bf16[4,512,768]{2,1,0:T(8,128)(2,1)}, f32[4,512,768]{2,1,0:T(8,128)}, bf16[4,512,768]{2,1,0:T(8,128...) while((s32[]{:T(128)}, f32[4,512,768]{2,1,0:T(8,128)}, ...), condition=%wide.region_9.10_spmd, body=%wide.region_8.9_spmd.sunk | while | flops 1233912576 | bytes 21243096 | solution.py:61
  305.5 3.5 bitcast_dynamic-update-slice_fusion.16
  309.0 4.2 bitcast_dynamic-update-slice_fusion.17
  317.6 3.4 bitcast_dynamic-update-slice_fusion.16
  321.1 4.2 bitcast_dynamic-update-slice_fusion.17
  329.8 3.5 bitcast_dynamic-update-slice_fusion.16
  333.3 4.2 bitcast_dynamic-update-slice_fusion.17
  342.0 3.5 bitcast_dynamic-update-slice_fusion.16
  345.5 4.2 bitcast_dynamic-update-slice_fusion.17
  351.7 109.5 %reduce-scatter.7.cloned.1.call-done = f32[512,768]{1,0:T(8,128)} async-done(((f32[2048,768]{1,0:T(8,128)}), f32[512,768]{1,0:T(8,128)}) %reduce-scatter.7.cloned.1.call-update) | async-done | bytes 1572880 | tf_op jit(solution)/shard_map/reduce_scatter | solution.py:180
  467.7 63.9 %all-gather.9.cloned.1.call-done = bf16[2048,768]{1,0:T(8,128)(2,1)} async-done(((bf16[512,768]{1,0:T(8,128)(2,1)}), bf16[2048,768]{1,0:T(8,128)(2,1)}) %all-gather.9.cloned.1.call-update) | async-done | bytes 3145744 | tf_op jit(solution)/shard_map/all_gather | solution.py:190
  536.5 3.1 broadcast.348
  539.7 79.0 %while.70 = (s32[]{:T(128)}, f32[2,768,768]{2,1,0:T(8,128)}, f32[2,768]{1,0:T(2,128)S(1)}, f32[2,768,768]{2,1,0:T(8,128)}, f32[4,512,768]{2,1,0:T(8,128)}, /*ind...) while((s32[]{:T(128)}, f32[2,768,768]{2,1,0:T(8,128)}, ...), condition=%wide.region_19.20_spmd, body=%wide.region_15.19_spmd.sunk | while | flops 2423784192 | bytes 36199780 | solution.py:90
  542.2 3.1 convert_reduce_fusion.9
  546.1 4.7 fusion.226
  552.1 5.3 fusion.227
  561.9 3.1 convert_reduce_fusion.9
  565.8 4.7 fusion.226
  571.8 5.3 fusion.227
  581.7 3.1 convert_reduce_fusion.9
  585.6 4.7 fusion.226
  591.7 5.3 fusion.227
  601.4 3.1 convert_reduce_fusion.9
  605.3 4.7 fusion.226
  611.4 5.3 fusion.227
  619.2 109.0 %reduce-scatter.9.cloned.1.call-done = f32[512,768]{1,0:T(8,128)} async-done(((f32[2048,768]{1,0:T(8,128)}), f32[512,768]{1,0:T(8,128)}) %reduce-scatter.9.cloned.1.call-update) | async-done | bytes 1572880 | tf_op jit(solution)/shard_map/reduce_scatter | solution.py:196
  728.3 2.9 fusion.146
  735.0 62.2 %all-gather.11.cloned.1.call-done = bf16[2048,768]{1,0:T(8,128)(2,1)} async-done(((bf16[512,768]{1,0:T(8,128)(2,1)}), bf16[2048,768]{1,0:T(8,128)(2,1)}) %all-gather.11.cloned.1.call-update) | async-done | bytes 3145744 | tf_op jit(solution)/shard_map/all_gather | solution.py:208
  800.4 95.7 %while.71 = (s32[]{:T(128)}, f32[2,3,768,192]{2,3,1,0:T(8,128)}, f32[2,2,192]{2,1,0:T(2,128)S(1)}, f32[2,192,768]{2,1,0:T(8,128)}, bf16[4,512,768]{2,1,0:T(8,128...) while((s32[]{:T(128)}, f32[2,3,768,192]{2,3,1,0:T(8,128)}, ...), condition=%wide.region_29.30_spmd, body=%wide.region_23.29_spmd.sunk | while | flops 1337720064 | bytes 39173132 | solution.py:279
  813.6 4.2 fusion.244
  819.4 3.2 fusion.245
  837.6 4.2 fusion.244
  843.3 3.2 fusion.245
  861.5 4.2 fusion.244
  867.2 3.2 fusion.245
  885.4 4.2 fusion.244
  891.2 3.2 fusion.245
  905.5 43.0 %all-reduce = (f32[2,2,768]{2,0,1:T(2,128)S(1)}, f32[2,2,768]{2,0,1:T(2,128)S(1)}, f32[2,2,768]{2,0,1:T(2,128)S(1)}) all-reduce(f32[2,2,768]{2,0,1:T(2,128)S(1)} %pad_maximum_fusion, f32[2,2,768]{2,0,1:T(2,128)S(1)} %pad_maximum_fusion.1, f32[2,2,768]{2,0,1:T(2,128)S(1)} %pad_maximum_fusion.2), channel_id=1, replica_groups=mesh['dp'=8,'tensor'=4] {'dp','tensor'}, use_global_device_ids=true, to_apply=%region_34.35 | all-reduce | flops 9216 | bytes 73728 | tf_op jit(solution)/shard_map/psum | solution.py:296
  950.3 24.0 %all-reduce.1 = (f32[2,2,192]{2,1,0:T(2,128)}, f32[2,768]{1,0:T(2,128)}) all-reduce(f32[2,2,192]{2,1,0:T(2,128)S(1)} %get-tuple-element.342, f32[2,768]{1,0:T(2,128)S(1)} %copy-done.25), channel_id=1, replica_groups=mesh['dp'=8,'tensor'=4] {'dp'}, use_global_device_ids=true, to_apply=%region_32.33 | all-reduce | flops 2304 | bytes 18432 | tf_op jit(solution)/shard_map/psum | solution.py:293
  976.7 173.9 %all-reduce.5.cloned.1.call-done = (f32[2,3,768,192]{2,3,1,0:T(8,128)}, f32[2,192,768]{2,1,0:T(8,128)}, f32[2,768,768]{2,1,0:T(8,128)}, f32[2,768,768]{2,1,0:T(8,128)}) async-done(((f32[2,3,768,192]{2,3,1,0:T(8,128)}, f32[2,192,768]{2,1,0:T(8,128)}, f32[2,768,768]{2,1,0:T(8,128)}, f32[2,768,768]{2,1,0:T(8,128)}), (f32[2,3,768,192]{2,3,1,0:T(8,128)}, f32[2,192,768]{2,1,0:T(8,128)}, f32[2,768,768]{2,1,0:T(8,128)}, ...) | async-done | bytes 14155792 | tf_op jit(solution)/shard_map/psum | solution.py:293
  1150.6 4.3 copy.275
  (527 shorter events, 165.3 us)
Async XLA Ops:
  7.2 68.6 %all-gather.5.cloned.1.call-start = ((), (), s32[]{:S(2)}) async-start(), calls=%async_computation.4 | async-start | bytes 3932160 | tf_op jit(solution)/shard_map/all_gather | solution.py:138
  7.9 220.2 %reduce-scatter.5.cloned.1.call-start = ((), (), s32[]{:S(2)}) async-start(), calls=%async_computation.5 | async-start | bytes 7864320 | tf_op jit(solution)/shard_map/reduce_scatter | solution.py:170
  119.5 177.2 %all-gather.7.cloned.1.call-start = ((), (), s32[]{:S(2)}) async-start(), calls=%async_computation.6 | async-start | bytes 3932160 | tf_op jit(solution)/shard_map/all_gather | solution.py:177
  120.6 109.9 %copy-start.17 = (f32[512,768]{1,0:T(8,128)}, f32[512,768]{1,0:T(8,128)S(1)}, u32[]{:S(2)}) copy-start(f32[512,768]{1,0:T(8,128)S(1)} %fusion.116) | copy-start | bytes 4718596
  230.2 501.0 %copy-start = (f32[512,768]{1,0:T(8,128)}, f32[512,768]{1,0:T(8,128)S(1)}, u32[]{:S(2)}) copy-start(f32[512,768]{1,0:T(8,128)S(1)} %get-tuple-element.566) | copy-start | bytes 4718596
  230.2 501.0 %copy-start.29 = (f32[512]{0:T(512)}, f32[512]{0:T(512)S(1)}, u32[]{:S(2)}) copy-start(f32[512]{0:T(512)S(1)} %broadcast_multiply_fusion.5) | copy-start | bytes 6148
  230.6 500.7 %copy-start.33 = (f32[512]{0:T(512)}, f32[512]{0:T(512)S(1)}, u32[]{:S(2)}) copy-start(f32[512]{0:T(512)S(1)} %add_rsqrt_fusion.1) | copy-start | bytes 6148
  232.5 228.7 %reduce-scatter.7.cloned.1.call-start = ((), (), s32[]{:S(2)}) async-start(), calls=%async_computation.7 | async-start | bytes 7864320 | tf_op jit(solution)/shard_map/reduce_scatter | solution.py:180
  309.0 4.2 copy-start.51
  333.3 4.2 copy-start.51
  351.6 179.9 %all-gather.9.cloned.1.call-start = ((), (), s32[]{:S(2)}) async-start(), calls=%async_computation.8 | async-start | bytes 3932160 | tf_op jit(solution)/shard_map/all_gather | solution.py:190
  467.5 260.8 %reduce-scatter.9.cloned.1.call-start = ((), (), s32[]{:S(2)}) async-start(), calls=%async_computation.9 | async-start | bytes 7864320 | tf_op jit(solution)/shard_map/reduce_scatter | solution.py:196
  545.3 5.5 copy-start.9
  552.1 5.3 copy-start.10
  552.1 5.3 copy-start.11
  565.0 5.5 copy-start.9
  571.8 5.3 copy-start.10
  571.8 5.3 copy-start.11
  584.8 5.5 copy-start.9
  591.6 5.3 copy-start.10
  591.6 5.3 copy-start.11
  604.5 5.5 copy-start.9
  611.4 5.3 copy-start.10
  611.4 5.3 copy-start.11
  619.2 177.9 %all-gather.11.cloned.1.call-start = ((), (), s32[]{:S(2)}) async-start(), calls=%async_computation.10 | async-start | bytes 3932160 | tf_op jit(solution)/shard_map/all_gather | solution.py:208
  733.1 241.2 %reduce-scatter.11.cloned.1.call-start = ((), (), s32[]{:S(2)}) async-start(), calls=%async_computation.11 | async-start | bytes 3932160 | tf_op jit(solution)/shard_map/reduce_scatter | solution.py:285
  800.4 5.4 copy-start.49
  800.4 5.8 copy-start.35
  813.6 4.4 copy-start.39
  818.0 4.5 copy-start.20
  824.3 5.5 copy-start.49
  824.3 5.8 copy-start.35
  837.6 4.4 copy-start.39
  841.9 4.5 copy-start.20
  848.2 5.5 copy-start.49
  848.2 5.8 copy-start.35
  861.5 4.4 copy-start.39
  865.8 4.5 copy-start.20
  872.1 5.5 copy-start.49
  872.1 5.8 copy-start.35
  885.4 4.4 copy-start.39
  889.8 4.5 copy-start.20
  896.0 254.5 %all-reduce.5.cloned.1.call-start = ((), (), s32[]{:S(2)}) async-start(), calls=%async_computation.12 | async-start | bytes 28311552 | tf_op jit(solution)/shard_map/psum | solution.py:293
  904.6 45.6 %copy-start.25 = (f32[2,768]{1,0:T(2,128)S(1)}, f32[2,768]{1,0:T(2,128)}, u32[]{:S(2)}) copy-start(f32[2,768]{1,0:T(2,128)} %copy-done.24) | copy-start | bytes 18436
  904.7 69.6 %copy-start.15 = (f32[512,768]{1,0:T(8,128)S(1)}, f32[512,768]{1,0:T(8,128)}, u32[]{:S(2)}) copy-start(f32[512,768]{1,0:T(8,128)} %get-tuple-element.534) | copy-start | bytes 4718596
  1150.6 4.4 copy-start.23
  1150.6 5.4 copy-start.21
  1155.0 4.2 slice-start
  (69 other events, 144.6 us)
Sparse Core Ops, SparseCore 0:
  9.6 66.1 all-gather.4
  118.7 109.3 reduce-scatter.4
  232.6 63.9 all-gather.6
  351.7 109.4 reduce-scatter.6
  467.6 63.9 all-gather.8
  618.8 109.4 reduce-scatter.8
  733.2 63.9 all-gather.10
  896.2 59.9 reduce-scatter.10
  961.4 189.1 all-reduce.4
where the time goes:
time: 1170 us
  waiting for transfers between devices  758 us (65%)
  matrix products  172 us (15%)
  local copies, waits for them, and re-layouts  73.4 us (6%)
  blocking collectives  67 us (6%)
  other arithmetic  50 us (4%)
  loops' own time  32.5 us (3%)
  between operations  14.2 us (1%)
    psum x1, waiting for transfers between devices, local(): lax.psum((acc_qkv, acc_qv, acc_out, up_total, ubias_total, down_total), '...  174 us
    reduce_scatter x1, waiting for transfers between devices, local(): lax.psum_scatter(ffn_parts.reshape(group_rows, -1), 'tensor', scatter_dim...  110 us
    reduce_scatter x1, waiting for transfers between devices, local(): lax.psum_scatter(ffn_back_parts.reshape(group_rows, -1), 'tensor', scatte...  109 us
    reduce_scatter x1, waiting for transfers between devices, local(): lax.psum_scatter(attn_parts.reshape(group_rows, -1), 'tensor', scatter_di...  107 us
    all_gather x1, waiting for transfers between devices, local(): gathered = lax.all_gather(inputs, 'tensor', axis=0, tiled=True)  67 us
    all_gather x1, waiting for transfers between devices, local(): gathered_norm = lax.all_gather(normed_low, 'tensor', axis=0, tiled=True)  64 us
    all_gather x1, waiting for transfers between devices, local(): gathered_two = lax.all_gather(d_two_low, 'tensor', axis=0, tiled=True)  63.9 us
    all_gather x1, waiting for transfers between devices, local(): lax.all_gather(d_one.astype(jnp.bfloat16), 'tensor', axis=0, tiled=True)  62.2 us
  transfers between devices with their start and end apart: 9, of which 8 were waited for; matrix products, arithmetic and copies ran while one was open for 1% of the time, Pallas kernels for 0%

commit v1 on v0

--- a/solution.py
+++ b/solution.py
@@ -9,6 +9,12 @@
 EPSILON = 1e-05
 SQRT_HALF = 0.7071067811865476
 INV_ROOT_TWO_PI = 0.3989422804014327
+
+
+def laid_out(blocks, dim):
+    shape = list(blocks.shape[1:])
+    shape[dim] *= blocks.shape[0]
+    return jnp.moveaxis(blocks, 0, dim).reshape(shape)
 
 
 def norm_forward(row_data, gain_rows, shift_rows):
@@ -187,7 +193,19 @@
     grad_out = cotangent.astype(jnp.float32)
     d_two = norm_backward(grad_out, gain_two, unit_two, inv_two)
     d_two_low = d_two.astype(jnp.bfloat16)
-    gathered_two = lax.all_gather(d_two_low, "tensor", axis=0, tiled=True)
+    size = lax.axis_size("tensor")
+    pairs = [(i, (i + 1) % size) for i in range(size)]
+    back = [(b, a) for a, b in pairs]
+    lower, upper = ([], [])
+    for k in range(size - 1):
+        if k % 2 == 0:
+            lower.append(lax.ppermute(lower[-1] if lower else d_two_low, "tensor", pairs))
+        else:
+            upper.append(lax.ppermute(upper[-1] if upper else d_two_low, "tensor", back))
+    tiles = jnp.stack([*lower[::-1], d_two_low, *upper])
+    shift = lax.axis_index("tensor") - len(lower)
+    tiles = tiles[(jnp.arange(size) - shift) % size]
+    gathered_two = laid_out(tiles, 0)
     two_blocks = gathered_two.reshape(n_blocks, block_rows, -1)
     (acc_up, acc_ubias, acc_down), ffn_back_parts = ffn_grad(
         w_up, up_bias, w_down, norm_blocks, two_blocks, kept_pre, kept_activ, block_kind

time: 1170 us -> 1170 us (level)
  waiting for transfers between devices: 758 us -> 732 us
  starting transfers between devices: 0.69 us -> 18.8 us
    all_gather x1 -> x0, waiting for transfers between devices: 63.9 us -> none  [local(): gathered_two = lax.all_gather(d_two_low, 'tensor', axis=0, tiled=True)]
    ppermute x0 -> x3, waiting for transfers between devices: none -> 36.7 us  [the longest x2 35.1 us: local(): lax.ppermute(lower[-1] if lower else d_two_low, 'tensor', pairs)]
    ppermute x0 -> x3, starting transfers between devices: none -> 18.3 us  [the longest x2 16 us: local(): lax.ppermute(lower[-1] if lower else d_two_low, 'tensor', pairs)]
  transfers between devices with their start and end apart: 9 -> 11, of which waited for: 8 -> 10; matrix products, arithmetic and copies ran while one was open for 1% -> 1% of each run, Pallas kernels for 0% -> 0%
where the time goes in v1:
time: 1170 us
  waiting for transfers between devices  732 us (63%)
  matrix products  172 us (15%)
  local copies, waits for them, and re-layouts  77.7 us (7%)
  blocking collectives  67 us (6%)
  other arithmetic  53.3 us (5%)
  loops' own time  32.5 us (3%)
  starting transfers between devices  18.8 us (2%)
  between operations  14.5 us (1%)
    psum x1, waiting for transfers between devices, local(): lax.psum((acc_qkv, acc_qv, acc_out, up_total, ubias_total, down_total), '...  174 us
    reduce_scatter x1, waiting for transfers between devices, local(): lax.psum_scatter(ffn_parts.reshape(group_rows, -1), 'tensor', scatter_dim...  110 us
    reduce_scatter x1, waiting for transfers between devices, local(): lax.psum_scatter(ffn_back_parts.reshape(group_rows, -1), 'tensor', scatte...  109 us
    reduce_scatter x1, waiting for transfers between devices, local(): lax.psum_scatter(attn_parts.reshape(group_rows, -1), 'tensor', scatter_di...  107 us
    all_gather x1, waiting for transfers between devices, local(): gathered = lax.all_gather(inputs, 'tensor', axis=0, tiled=True)  67 us
    all_gather x1, waiting for transfers between devices, local(): gathered_norm = lax.all_gather(normed_low, 'tensor', axis=0, tiled=True)  64 us
    all_gather x1, waiting for transfers between devices, local(): lax.all_gather(d_one.astype(jnp.bfloat16), 'tensor', axis=0, tiled=True)  62.2 us
    psum x1, blocking collectives, local(): lax.psum((rbias_grads, gain_grads, shift_grads), ('dp', 'tensor'))  43 us
  transfers between devices with their start and end apart: 11, of which 10 were waited for; matrix products, arithmetic and copies ran while one was open for 1% of the time, Pallas kernels for 0%

profile of v1, /device:TPU:0, one launch (start us, length us, event | category | flops | bytes accessed | tf_op | source)
XLA Modules:
  0.0 1167.5 jit_solution(13195394639864961860)
XLA Ops:
  8.8 67.0 %all-gather.4.cloned.1.call-done = bf16[2048,768]{1,0:T(8,128)(2,1)} async-done(((bf16[512,768]{1,0:T(8,128)(2,1)}), bf16[2048,768]{1,0:T(8,128)(2,1)}) %all-gather.4.cloned.1.call-update) | async-done | bytes 3145744 | tf_op jit(solution)/shard_map/all_gather | solution.py:144
  75.8 3.2 broadcast.411.clone
  79.0 39.6 %while.68 = (s32[]{:T(128)}, bf16[4,3,512,192]{2,3,1,0:T(8,128)(2,1)}, f32[4,4,3,128]{3,2,1,0:T(4,128)S(1)}, bf16[4,512,192]{1,2,0:T(8,128)(2,1)S(1)}, f32[4,512...) while((s32[]{:T(128)}, ...), condition=%wide.region_3.4_spmd, body=%wide.region_0.3_spmd.sunk | while | flops 658340736 | bytes 15210975 | solution.py:173
  120.6 107.5 %reduce-scatter.5.cloned.1.call-done = f32[512,768]{1,0:T(8,128)} async-done(((f32[2048,768]{1,0:T(8,128)}), f32[512,768]{1,0:T(8,128)}) %reduce-scatter.5.cloned.1.call-update) | async-done | bytes 1572880 | tf_op jit(solution)/shard_map/reduce_scatter | solution.py:176
  232.6 64.0 %all-gather.6.cloned.1.call-done = bf16[2048,768]{1,0:T(8,128)(2,1)} async-done(((bf16[512,768]{1,0:T(8,128)(2,1)}), bf16[2048,768]{1,0:T(8,128)(2,1)}) %all-gather.6.cloned.1.call-update) | async-done | bytes 3145744 | tf_op jit(solution)/shard_map/all_gather | solution.py:183
  296.6 3.2 broadcast.411.clone.1
  299.8 3.1 broadcast.411.clone.2
  303.0 48.6 %while.69 = (s32[]{:T(128)}, f32[4,512,768]{2,1,0:T(8,128)}, bf16[4,512,768]{2,1,0:T(8,128)(2,1)}, f32[4,512,768]{2,1,0:T(8,128)}, bf16[4,512,768]{2,1,0:T(8,128...) while((s32[]{:T(128)}, f32[4,512,768]{2,1,0:T(8,128)}, ...), condition=%wide.region_9.10_spmd, body=%wide.region_8.9_spmd.sunk | while | flops 1233912576 | bytes 21243096 | solution.py:67
  305.5 3.5 bitcast_dynamic-update-slice_fusion.16
  309.0 4.2 bitcast_dynamic-update-slice_fusion.17
  317.6 3.4 bitcast_dynamic-update-slice_fusion.16
  321.1 4.2 bitcast_dynamic-update-slice_fusion.17
  329.8 3.5 bitcast_dynamic-update-slice_fusion.16
  333.3 4.2 bitcast_dynamic-update-slice_fusion.17
  342.0 3.5 bitcast_dynamic-update-slice_fusion.16
  345.5 4.2 bitcast_dynamic-update-slice_fusion.17
  351.7 109.5 %reduce-scatter.7.cloned.1.call-done = f32[512,768]{1,0:T(8,128)} async-done(((f32[2048,768]{1,0:T(8,128)}), f32[512,768]{1,0:T(8,128)}) %reduce-scatter.7.cloned.1.call-update) | async-done | bytes 1572880 | tf_op jit(solution)/shard_map/reduce_scatter | solution.py:186
  471.3 18.7 %collective-permute-done = bf16[512,768]{1,0:T(8,128)(2,1)} collective-permute-done((bf16[512,768]{1,0:T(8,128)(2,1)}, bf16[512,768]{1,0:T(8,128)(2,1)}, u32[]{:S(2)}, u32[]{:S(2)}) %collective-permute-start) | collective-permute-done | bytes 786464 | tf_op jit(solution)/shard_map/ppermute | solution.py:202
  490.0 14.5 %collective-permute-start.1 = (bf16[512,768]{1,0:T(8,128)(2,1)}, bf16[512,768]{1,0:T(8,128)(2,1)}, u32[]{:S(2)}, u32[]{:S(2)}) collective-permute-start(bf16[512,768]{1,0:T(8,128)(2,1)} %collective-permute-done), channel_id=1, source_target_pairs={{0,1},{1,2},{2,3},{3,0},{4,5},{5,6},{6,7},{7,4},{8,9},{9,10},{10,1... | collective-permute-start | bytes 2359304 | tf_op jit(solution)/shard_map/ppermute | solution.py:202
  506.2 16.3 %collective-permute-done.1 = bf16[512,768]{1,0:T(8,128)(2,1)} collective-permute-done((bf16[512,768]{1,0:T(8,128)(2,1)}, bf16[512,768]{1,0:T(8,128)(2,1)}, u32[]{:S(2)}, u32[]{:S(2)}) %collective-permute-start.1) | collective-permute-done | bytes 786464 | tf_op jit(solution)/shard_map/ppermute | solution.py:202
  522.5 3.2 pad_maximum_fusion
  525.7 4.4 gather_fusion
  535.1 3.1 broadcast.411
  538.2 79.0 %while.70 = (s32[]{:T(128)}, f32[2,768,768]{2,1,0:T(8,128)}, f32[2,768]{1,0:T(2,128)S(1)}, f32[2,768,768]{2,1,0:T(8,128)}, f32[4,512,768]{2,1,0:T(8,128)}, /*ind...) while((s32[]{:T(128)}, f32[2,768,768]{2,1,0:T(8,128)}, ...), condition=%wide.region_19.20_spmd, body=%wide.region_15.19_spmd.sunk | while | flops 2423784192 | bytes 36199780 | solution.py:96
  544.6 4.7 fusion.228
  550.7 5.3 fusion.229
  560.4 3.1 convert_reduce_fusion.9
  564.3 4.7 fusion.228
  570.4 5.3 fusion.229
  584.1 4.7 fusion.228
  590.2 5.3 fusion.229
  603.9 4.7 fusion.228
  609.9 5.3 fusion.229
  617.8 109.5 %reduce-scatter.9.cloned.1.call-done = f32[512,768]{1,0:T(8,128)} async-done(((f32[2048,768]{1,0:T(8,128)}), f32[512,768]{1,0:T(8,128)}) %reduce-scatter.9.cloned.1.call-update) | async-done | bytes 1572880 | tf_op jit(solution)/shard_map/reduce_scatter | solution.py:214
  734.0 62.2 %all-gather.8.cloned.1.call-done = bf16[2048,768]{1,0:T(8,128)(2,1)} async-done(((bf16[512,768]{1,0:T(8,128)(2,1)}), bf16[2048,768]{1,0:T(8,128)(2,1)}) %all-gather.8.cloned.1.call-update) | async-done | bytes 3145744 | tf_op jit(solution)/shard_map/all_gather | solution.py:226
  799.4 95.7 %while.71 = (s32[]{:T(128)}, f32[2,3,768,192]{2,3,1,0:T(8,128)}, f32[2,2,192]{2,1,0:T(2,128)S(1)}, f32[2,192,768]{2,1,0:T(8,128)}, bf16[4,512,768]{2,1,0:T(8,128...) while((s32[]{:T(128)}, f32[2,3,768,192]{2,3,1,0:T(8,128)}, ...), condition=%wide.region_29.30_spmd, body=%wide.region_23.29_spmd.sunk | while | flops 1337720064 | bytes 39173132 | solution.py:297
  812.7 4.2 fusion.246
  818.4 3.2 fusion.247
  836.6 4.2 fusion.246
  842.3 3.2 fusion.247
  860.5 4.2 fusion.246
  866.2 3.2 fusion.247
  884.4 4.2 fusion.246
  890.2 3.2 fusion.247
  904.5 43.0 %all-reduce = (f32[2,2,768]{2,0,1:T(2,128)S(1)}, f32[2,2,768]{2,0,1:T(2,128)S(1)}, f32[2,2,768]{2,0,1:T(2,128)S(1)}) all-reduce(f32[2,2,768]{2,0,1:T(2,128)S(1)} %pad_maximum_fusion.1, f32[2,2,768]{2,0,1:T(2,128)S(1)} %pad_maximum_fusion.2, f32[2,2,768]{2,0,1:T(2,128)S(1)} %pad_maximum_fusion.3), channel_id=1, replica_groups=mesh['dp'=8,'tensor'=4] {'dp','tensor'}, use_global_device_ids=true, to_apply=%region_34.35 | all-reduce | flops 9216 | bytes 73728 | tf_op jit(solution)/shard_map/psum | solution.py:314
  949.3 24.0 %all-reduce.1 = (f32[2,2,192]{2,1,0:T(2,128)}, f32[2,768]{1,0:T(2,128)}) all-reduce(f32[2,2,192]{2,1,0:T(2,128)S(1)} %get-tuple-element.342, f32[2,768]{1,0:T(2,128)S(1)} %copy-done.25), channel_id=1, replica_groups=mesh['dp'=8,'tensor'=4] {'dp'}, use_global_device_ids=true, to_apply=%region_32.33 | all-reduce | flops 2304 | bytes 18432 | tf_op jit(solution)/shard_map/psum | solution.py:311
  975.8 173.8 %all-reduce.5.cloned.1.call-done = (f32[2,3,768,192]{2,3,1,0:T(8,128)}, f32[2,192,768]{2,1,0:T(8,128)}, f32[2,768,768]{2,1,0:T(8,128)}, f32[2,768,768]{2,1,0:T(8,128)}) async-done(((f32[2,3,768,192]{2,3,1,0:T(8,128)}, f32[2,192,768]{2,1,0:T(8,128)}, f32[2,768,768]{2,1,0:T(8,128)}, f32[2,768,768]{2,1,0:T(8,128)}), (f32[2,3,768,192]{2,3,1,0:T(8,128)}, f32[2,192,768]{2,1,0:T(8,128)}, f32[2,768,768]{2,1,0:T(8,128)}, ...) | async-done | bytes 14155792 | tf_op jit(solution)/shard_map/psum | solution.py:311
  1149.6 4.3 copy.275
  (534 shorter events, 182.8 us)
Async XLA Ops:
  7.2 68.6 %all-gather.4.cloned.1.call-start = ((), (), s32[]{:S(2)}) async-start(), calls=%async_computation.4 | async-start | bytes 3932160 | tf_op jit(solution)/shard_map/all_gather | solution.py:144
  7.9 220.2 %reduce-scatter.5.cloned.1.call-start = ((), (), s32[]{:S(2)}) async-start(), calls=%async_computation.5 | async-start | bytes 7864320 | tf_op jit(solution)/shard_map/reduce_scatter | solution.py:176
  119.5 177.2 %all-gather.6.cloned.1.call-start = ((), (), s32[]{:S(2)}) async-start(), calls=%async_computation.6 | async-start | bytes 3932160 | tf_op jit(solution)/shard_map/all_gather | solution.py:183
  120.6 109.9 %copy-start.17 = (f32[512,768]{1,0:T(8,128)}, f32[512,768]{1,0:T(8,128)S(1)}, u32[]{:S(2)}) copy-start(f32[512,768]{1,0:T(8,128)S(1)} %fusion.116) | copy-start | bytes 4718596
  230.2 500.0 %copy-start = (f32[512,768]{1,0:T(8,128)}, f32[512,768]{1,0:T(8,128)S(1)}, u32[]{:S(2)}) copy-start(f32[512,768]{1,0:T(8,128)S(1)} %get-tuple-element.566) | copy-start | bytes 4718596
  230.2 500.0 %copy-start.29 = (f32[512]{0:T(512)}, f32[512]{0:T(512)S(1)}, u32[]{:S(2)}) copy-start(f32[512]{0:T(512)S(1)} %broadcast_multiply_fusion.5) | copy-start | bytes 6148
  230.6 499.7 %copy-start.33 = (f32[512]{0:T(512)}, f32[512]{0:T(512)S(1)}, u32[]{:S(2)}) copy-start(f32[512]{0:T(512)S(1)} %add_rsqrt_fusion.1) | copy-start | bytes 6148
  232.5 228.7 %reduce-scatter.7.cloned.1.call-start = ((), (), s32[]{:S(2)}) async-start(), calls=%async_computation.7 | async-start | bytes 7864320 | tf_op jit(solution)/shard_map/reduce_scatter | solution.py:186
  351.6 375.7 %reduce-scatter.9.cloned.1.call-start = ((), (), s32[]{:S(2)}) async-start(), calls=%async_computation.8 | async-start | bytes 7864320 | tf_op jit(solution)/shard_map/reduce_scatter | solution.py:214
  467.4 22.6 %collective-permute-start = (bf16[512,768]{1,0:T(8,128)(2,1)}, bf16[512,768]{1,0:T(8,128)(2,1)}, u32[]{:S(2)}, u32[]{:S(2)}) collective-permute-start(bf16[512,768]{1,0:T(8,128)(2,1)} %get-tuple-element.536), channel_id=1, source_target_pairs={{0,1},{1,2},{2,3},{3,0},{4,5},{5,6},{6,7},{7,4},{8,9},{9,10},{10,1... | collective-permute-start | bytes 2359304 | tf_op jit(solution)/shard_map/ppermute | solution.py:202
  468.9 37.3 %collective-permute-start.2 = (bf16[512,768]{1,0:T(8,128)(2,1)}, bf16[512,768]{1,0:T(8,128)(2,1)}, u32[]{:S(2)}, u32[]{:S(2)}) collective-permute-start(bf16[512,768]{1,0:T(8,128)(2,1)} %get-tuple-element.536), channel_id=1, source_target_pairs={{1,0},{2,1},{3,2},{0,3},{5,4},{6,5},{7,6},{4,7},{9,8},{10,9},{11,1... | collective-permute-start | bytes 2359304 | tf_op jit(solution)/shard_map/ppermute | solution.py:204
  490.0 32.5 %collective-permute-start.1 = (bf16[512,768]{1,0:T(8,128)(2,1)}, bf16[512,768]{1,0:T(8,128)(2,1)}, u32[]{:S(2)}, u32[]{:S(2)}) collective-permute-start(bf16[512,768]{1,0:T(8,128)(2,1)} %collective-permute-done), channel_id=1, source_target_pairs={{0,1},{1,2},{2,3},{3,0},{4,5},{5,6},{6,7},{7,4},{8,9},{9,10},{10,1... | collective-permute-start | bytes 2359304 | tf_op jit(solution)/shard_map/ppermute | solution.py:202
  543.8 5.5 copy-start.9
  550.6 5.3 copy-start.10
  550.6 5.3 copy-start.11
  563.5 5.5 copy-start.9
  570.3 5.3 copy-start.10
  570.4 5.3 copy-start.11
  583.4 5.5 copy-start.9
  590.2 5.3 copy-start.10
  590.2 5.3 copy-start.11
  603.1 5.5 copy-start.9
  609.9 5.3 copy-start.10
  609.9 5.3 copy-start.11
  617.8 178.4 %all-gather.8.cloned.1.call-start = ((), (), s32[]{:S(2)}) async-start(), calls=%async_computation.9 | async-start | bytes 3932160 | tf_op jit(solution)/shard_map/all_gather | solution.py:226
  732.1 241.2 %reduce-scatter.11.cloned.1.call-start = ((), (), s32[]{:S(2)}) async-start(), calls=%async_computation.10 | async-start | bytes 3932160 | tf_op jit(solution)/shard_map/reduce_scatter | solution.py:303
  799.4 5.4 copy-start.49
  799.4 5.8 copy-start.35
  812.7 4.4 copy-start.39
  817.0 4.5 copy-start.20
  823.3 5.5 copy-start.49
  823.3 5.8 copy-start.35
  836.6 4.4 copy-start.39
  841.0 4.5 copy-start.20
  847.2 5.5 copy-start.49
  847.2 5.8 copy-start.35
  860.5 4.4 copy-start.39
  864.9 4.5 copy-start.20
  871.1 5.5 copy-start.49
  871.2 5.8 copy-start.35
  884.4 4.4 copy-start.39
  888.8 4.5 copy-start.20
  895.1 254.5 %all-reduce.5.cloned.1.call-start = ((), (), s32[]{:S(2)}) async-start(), calls=%async_computation.11 | async-start | bytes 28311552 | tf_op jit(solution)/shard_map/psum | solution.py:311
  903.7 45.7 %copy-start.25 = (f32[2,768]{1,0:T(2,128)S(1)}, f32[2,768]{1,0:T(2,128)}, u32[]{:S(2)}) copy-start(f32[2,768]{1,0:T(2,128)} %copy-done.24) | copy-start | bytes 18436
  903.7 69.7 %copy-start.15 = (f32[512,768]{1,0:T(8,128)S(1)}, f32[512,768]{1,0:T(8,128)}, u32[]{:S(2)}) copy-start(f32[512,768]{1,0:T(8,128)} %get-tuple-element.534) | copy-start | bytes 4718596
  1149.6 4.4 copy-start.23
  1149.6 5.4 copy-start.21
  1154.0 4.2 slice-start
  (71 other events, 152.9 us)
Sparse Core Ops, SparseCore 0:
  9.6 66.1 all-gather.3
  118.7 109.3 reduce-scatter.4
  232.6 63.9 all-gather.5
  351.7 109.4 reduce-scatter.6
  617.3 109.8 reduce-scatter.8
  732.2 63.9 all-gather.7
  895.2 59.9 reduce-scatter.10
  960.4 189.1 all-reduce.4
